TPU v7x, 256 devices: a whole 4x4x8 slice. The times are simulated.
256 devices in a mesh: chan: 8 (over z_hi, x), tm: 16 (over z_lo, y), dp: 2 (over core).
Axes of the slice: x: 4, y: 4, z: 8 (z_hi: 2, z_lo: 4; z = z_hi * 4 + z_lo), core: 2. Of those that a mesh axis runs over, the one named last changes fastest.
Arguments:
- contexts: bfloat16 [512, 4, 16384], P('tm', 'dp', 'chan'), may hold values from -6 to 6
- cotangent: bfloat16 [512, 4, 16384], P('tm', 'dp', 'chan'), may hold values from -6 to 6
- w_in: bfloat16 [16384, 8192], P('chan', 'tm'), may hold values from -0.046875 to 0.046875
- w_out: bfloat16 [8192, 16384], P('tm', 'chan'), may hold values from -0.0625 to 0.0625
- time_weight: bfloat16 [512, 512], replicated, may hold values from -0.25 to 0.25
Outputs:
- grad_contexts: bfloat16 [512, 4, 16384], P('tm', 'dp', 'chan')
- grad_w_in: float32 [16384, 8192], P('chan', ('tm', 'dp'))
- grad_w_out: float32 [8192, 16384], P(('tm', 'dp'), 'chan')
- grad_time: float32 [512, 512], replicated
All inputs are finite; a program needn't handle non-finite values.
Results may differ from a plain program's by a relative error of at most 0.0057.
Values may be sent and summed in bfloat16 or wider, within the bound.
No kernel may reach another device: no remote copies, remote signals or barrier semaphores. Data moves between devices by JAX's collectives and lax.ppermute only.
A program may use at most 192 MiB of HBM per device.

v0:
```python
import math
import jax
import jax.numpy as jnp
from jax import lax
from jax.sharding import PartitionSpec as P

tanh_scale = math.sqrt(2.0 / math.pi)
cubic_term = 0.044715


def gelu_pair(value):
    inner = jnp.tanh(tanh_scale * (value + cubic_term * value * value * value))
    result = 0.5 * value * (1.0 + inner)
    slope = 0.5 * (1.0 + inner) + 0.5 * value * (1.0 - inner * inner) * tanh_scale * (
        1.0 + 3.0 * cubic_term * value * value
    )
    return (result, slope)


def hidden_finish(hidden_pre, hidden_grad):
    act_hidden, slope_hidden = gelu_pair(hidden_pre)
    return (act_hidden.astype(jnp.bfloat16), (hidden_grad * slope_hidden).astype(jnp.bfloat16))


def on_device(contexts, cotangent, w_in, w_out, time_weight):
    local_len, batch_dev, width_dev = contexts.shape
    whole_x, whole_dy = (
        lax.all_gather(contexts, "tm", axis=0, tiled=True),
        lax.all_gather(cotangent, "tm", axis=0, tiled=True),
    )
    length = whole_x.shape[0]
    flat_x = whole_x.reshape(length, batch_dev * width_dev)
    pre_time = jnp.dot(time_weight, flat_x, preferred_element_type=jnp.float32)
    act_time, slope_time = gelu_pair(pre_time)
    mixed = (
        (flat_x.astype(jnp.float32) + act_time)
        .astype(jnp.bfloat16)
        .reshape(length * batch_dev, width_dev)
    )
    grad_rows = whole_dy.reshape(length * batch_dev, width_dev)
    hidden_part = jnp.dot(mixed, w_in, preferred_element_type=jnp.float32)
    hgrad_part = jnp.einsum("rc,hc->rh", grad_rows, w_out, preferred_element_type=jnp.float32)
    hidden_pre, hidden_grad = lax.psum((hidden_part, hgrad_part), "chan")
    activation, pre_grad = hidden_finish(hidden_pre, hidden_grad)
    win_part = jnp.einsum("rc,rh->ch", mixed, pre_grad, preferred_element_type=jnp.float32)
    wout_part = jnp.einsum("rh,rc->hc", activation, grad_rows, preferred_element_type=jnp.float32)
    grad_w_in, grad_w_out = (
        lax.psum_scatter(win_part, "dp", scatter_dimension=1, tiled=True),
        lax.psum_scatter(wout_part, "dp", scatter_dimension=0, tiled=True),
    )
    position = lax.axis_index("tm")
    my_rows = local_len * batch_dev
    feature_sum = lax.psum_scatter(
        jnp.einsum("rh,ch->rc", pre_grad, w_in, preferred_element_type=jnp.float32),
        "tm",
        scatter_dimension=0,
        tiled=True,
    )
    own_dy = cotangent.reshape(my_rows, width_dev)
    mixed_grad = (own_dy.astype(jnp.float32) + feature_sum).reshape(
        local_len, batch_dev * width_dev
    )
    own_slope = lax.dynamic_slice_in_dim(slope_time, position * local_len, local_len, 0)
    own_gate = (mixed_grad * own_slope).astype(jnp.bfloat16)
    all_gate = lax.all_gather(own_gate, "tm", axis=0, tiled=True)
    own_columns = lax.dynamic_slice_in_dim(time_weight, position * local_len, local_len, 1)
    back = jnp.einsum("tl,tk->lk", own_columns, all_gate, preferred_element_type=jnp.float32)
    grad_contexts = (
        (mixed_grad + back).reshape(local_len, batch_dev, width_dev).astype(jnp.bfloat16)
    )
    time_part = jnp.einsum("tk,lk->tl", own_gate, flat_x, preferred_element_type=jnp.float32)
    time_rows = lax.psum(time_part, ("chan", "dp"))
    grad_time = lax.all_gather(time_rows, "tm", axis=0, tiled=True)
    return (grad_contexts, grad_w_in, grad_w_out, grad_time)


def solution(mesh):
    return jax.shard_map(
        on_device,
        mesh=mesh,
        in_specs=(
            P("tm", "dp", "chan"),
            P("tm", "dp", "chan"),
            P("chan", "tm"),
            P("tm", "chan"),
            P(),
        ),
        out_specs=(P("tm", "dp", "chan"), P("chan", ("tm", "dp")), P(("tm", "dp"), "chan"), P()),
        check_vma=False,
    )
```

profile of v0, /device:TPU:1, one launch (start us, length us, event | category | flops | bytes accessed | tf_op | source)
XLA Modules:
  0.0 907.4 jit_solution(18198101720754820874)
XLA Ops:
  7.2 0.0 copy-start
  7.2 0.0 all-gather.7.cloned.1.call-start
  7.2 0.7 all-gather.7.cloned.1.call-update
  7.9 0.0 all-gather.5.cloned.1.call-start
  8.0 0.7 all-gather.5.cloned.1.call-update
  8.7 0.0 all-reduce.6.cloned.1.call-start
  8.7 83.0 %all-gather.7.cloned.1.call-done = bf16[512,2,2048]{2,1,0:T(2,128)(2,1)} async-done(((bf16[32,2,2048]{2,1,0:T(2,128)(2,1)}), bf16[512,2,2048]{2,1,0:T(2,128)(2,1)}) %all-gather.7.cloned.1.call-update) | async-done | bytes 4194320 | tf_op jit(solution)/shard_map/all_gather | solution.py:28
  91.7 0.0 copy-start.9
  91.7 4.6 copy.9
  96.4 0.0 copy-start.2
  96.4 0.0 copy-done.9
  96.4 14.4 %fusion.1 = (f32[512,4096]{1,0:T(8,128)}, f32[512,4096]{1,0:T(8,128)}, bf16[512,4096]{1,0:T(8,128)(2,1)}, f32[512,4096]{1,0:T(8,128)}, f32[512,4096]{1,0:T(8,128)}) fusion(bf16[512,4096]{1,0:T(8,128)(2,1)S(1)} %bitcast.16, bf16[512,512]{1,0:T(8,128)(2,1)S(1)} %copy-done.9), kind=kOutput, calls=%fused_computation.2 | convolution fusion | flops 2170552320 | bytes 42467328 | tf_op jit(solution)/shard_map/dot_general | solution.py:33
  110.7 0.0 copy-done.2
  110.7 7.1 reshape.27
  117.9 61.4 %all-gather.5.cloned.1.call-done = bf16[512,2,2048]{2,1,0:T(2,128)(2,1)} async-done(((bf16[32,2,2048]{2,1,0:T(2,128)(2,1)}), bf16[512,2,2048]{2,1,0:T(2,128)(2,1)}) %all-gather.5.cloned.1.call-update) | async-done | bytes 4194320 | tf_op jit(solution)/shard_map/all_gather | solution.py:29
  179.3 7.2 reshape.25
  186.4 0.0 copy-start.3
  186.4 6.7 fusion.28
  193.1 0.0 copy-done
  193.1 0.0 copy-done.3
  193.1 3.7 fusion.29
  196.8 0.0 all-reduce.6.cloned.1.call-update
  196.8 0.2 reduce-scatter.4.cloned.1.call-start
  197.0 198.9 %all-reduce.6.cloned.1.call-done = (f32[1024,512]{1,0:T(8,128)}, f32[1024,512]{1,0:T(8,128)}) async-done(((f32[1024,512]{1,0:T(8,128)}, f32[1024,512]{1,0:T(8,128)}), (f32[1024,512]{1,0:T(8,128)}, f32[1024,512]{1,0:T(8,128)})) %all-reduce.6.cloned.1.call-update) | async-done | bytes 4194320 | tf_op jit(solution)/shard_map/psum | solution.py:43
  395.9 3.5 fusion.9
  399.5 0.0 copy-start.6
  399.5 1.0 copy-done.6
  400.4 5.6 fusion.30
  406.0 0.0 copy-start.8
  406.0 0.0 reduce-scatter.4.cloned.1.call-update
  406.1 0.0 all-reduce.4.cloned.1.call-start
  406.1 0.9 copy-done.8
  407.0 0.1 reshape.29
  407.1 101.0 %reduce-scatter.4.cloned.1.call-done = f32[64,2048]{1,0:T(8,128)} async-done(((f32[1024,2048]{1,0:T(8,128)}), f32[64,2048]{1,0:T(8,128)}) %reduce-scatter.4.cloned.1.call-update) | async-done | bytes 524304 | tf_op jit(solution)/shard_map/reduce_scatter | solution.py:53
  508.0 1.1 add.58
  509.1 0.2 reshape.28
  509.3 1.7 fusion.19
  511.0 0.0 copy-start.4
  511.1 0.0 copy-start.7
  511.1 4.3 fusion.32
  515.4 0.0 copy-done.4
  515.4 0.0 all-reduce.4.cloned.1.call-update
  515.4 0.0 all-gather.11.cloned.1.call-start
  515.4 170.7 %all-reduce.4.cloned.1.call-done = f32[32,512]{1,0:T(8,128)} async-done(((f32[32,512]{1,0:T(8,128)}), f32[32,512]{1,0:T(8,128)}) %all-reduce.4.cloned.1.call-update) | async-done | bytes 65552 | tf_op jit(solution)/shard_map/psum | solution.py:72
  686.1 0.0 all-gather.11.cloned.1.call-update
  686.1 0.0 all-gather.9.cloned.1.call-start
  686.2 0.7 all-gather.9.cloned.1.call-update
  686.9 0.0 reduce-scatter.6.cloned.1.call-start
  686.9 0.0 copy-done.7
  686.9 6.5 fusion.31
  693.5 0.0 copy-start.5
  693.5 0.0 reduce-scatter.6.cloned.1.call-update
  693.5 0.0 reduce-scatter.8.cloned.1.call-start
  693.5 1.5 copy-done.5
  695.0 6.7 fusion.10
  701.8 0.0 reduce-scatter.8.cloned.1.call-update
  701.8 56.8 %all-gather.11.cloned.1.call-done = f32[512,512]{1,0:T(8,128)} async-done(((f32[32,512]{1,0:T(8,128)}), f32[512,512]{1,0:T(8,128)}) %all-gather.11.cloned.1.call-update) | async-done | bytes 1048592 | tf_op jit(solution)/shard_map/all_gather | solution.py:73
  758.6 89.3 %all-gather.9.cloned.1.call-done = bf16[512,4096]{1,0:T(8,128)(2,1)} async-done(((bf16[32,4096]{1,0:T(8,128)(2,1)}), bf16[512,4096]{1,0:T(8,128)(2,1)}) %all-gather.9.cloned.1.call-update) | async-done | bytes 4194320 | tf_op jit(solution)/shard_map/all_gather | solution.py:65
  848.0 3.3 fusion.2
  851.2 0.9 convert_element_type.34
  852.1 24.6 %reduce-scatter.6.cloned.1.call-done = f32[2048,256]{1,0:T(8,128)} async-done(((f32[2048,512]{1,0:T(8,128)}), f32[2048,256]{1,0:T(8,128)}) %reduce-scatter.6.cloned.1.call-update) | async-done | bytes 2097168 | tf_op jit(solution)/shard_map/reduce_scatter | solution.py:48
  876.7 21.9 %reduce-scatter.8.cloned.1.call-done = f32[256,2048]{1,0:T(8,128)} async-done(((f32[512,2048]{1,0:T(8,128)}), f32[256,2048]{1,0:T(8,128)}) %reduce-scatter.8.cloned.1.call-update) | async-done | bytes 2097168 | tf_op jit(solution)/shard_map/reduce_scatter | solution.py:49
  898.6 2.3 copy.14
  900.9 0.0 copy-done.1
  (1 shorter events, 0.0 us)
Async XLA Ops:
  7.2 186.0 %copy-start = (bf16[2048,512]{1,0:T(8,128)(2,1)S(1)}, bf16[2048,512]{1,0:T(8,128)(2,1)}, u32[]{:S(2)}) copy-start(bf16[2048,512]{1,0:T(8,128)(2,1)} %param.7) | copy-start | bytes 6291460
  7.2 84.5 %all-gather.7.cloned.1.call-start = ((), (), s32[]{:S(2)}) async-start(), calls=%async_computation.4 | async-start | bytes 4456448 | tf_op jit(solution)/shard_map/all_gather | solution.py:28
  7.9 171.3 %all-gather.5.cloned.1.call-start = ((), (), s32[]{:S(2)}) async-start(), calls=%async_computation.3 | async-start | bytes 4456448 | tf_op jit(solution)/shard_map/all_gather | solution.py:29
  8.7 387.2 %all-reduce.6.cloned.1.call-start = ((), (), s32[]{:S(2)}) async-start(), calls=%async_computation.11 | async-start | bytes 8388608 | tf_op jit(solution)/shard_map/psum | solution.py:43
  91.7 4.7 copy-start.9
  96.4 14.4 %copy-start.2 = (bf16[64,8,2,2048]{3,1,2,0:T(8,128)(2,1)}, bf16[64,8,2,2048]{3,1,2,0:T(8,128)(2,1)S(1)}, u32[]{:S(2)}) copy-start(bf16[64,8,2,2048]{3,1,2,0:T(8,128)(2,1)S(1)} %copy.9) | copy-start | bytes 12582916
  186.4 6.7 copy-start.3
  196.8 311.2 %reduce-scatter.4.cloned.1.call-start = ((), (), s32[]{:S(2)}) async-start(), calls=%async_computation.5 | async-start | bytes 8912896 | tf_op jit(solution)/shard_map/reduce_scatter | solution.py:53
  399.5 1.0 copy-start.6
  406.0 0.9 copy-start.8
  406.1 280.1 %all-reduce.4.cloned.1.call-start = ((), (), s32[]{:S(2)}) async-start(), calls=%async_computation.9 | async-start | bytes 131072 | tf_op jit(solution)/shard_map/psum | solution.py:72
  511.0 4.3 copy-start.4
  511.1 175.9 %copy-start.7 = (bf16[1024,512]{1,0:T(8,128)(2,1)S(1)}, bf16[1024,512]{1,0:T(8,128)(2,1)}, u32[]{:S(2)}) copy-start(bf16[1024,512]{1,0:T(8,128)(2,1)} %copy-done.6) | copy-start | bytes 3145732
  515.4 243.2 %all-gather.11.cloned.1.call-start = ((), (), s32[]{:S(2)}) async-start(), calls=%async_computation.10 | async-start | bytes 1114112 | tf_op jit(solution)/shard_map/all_gather | solution.py:73
  686.1 161.8 %all-gather.9.cloned.1.call-start = ((), (), s32[]{:S(2)}) async-start(), calls=%async_computation.6 | async-start | bytes 4456448 | tf_op jit(solution)/shard_map/all_gather | solution.py:65
  686.9 189.9 %reduce-scatter.6.cloned.1.call-start = ((), (), s32[]{:S(2)}) async-start(), calls=%async_computation.7 | async-start | bytes 6291456 | tf_op jit(solution)/shard_map/reduce_scatter | solution.py:48
  693.5 1.6 copy-start.5
  693.5 205.2 %reduce-scatter.8.cloned.1.call-start = ((), (), s32[]{:S(2)}) async-start(), calls=%async_computation.8 | async-start | bytes 6291456 | tf_op jit(solution)/shard_map/reduce_scatter | solution.py:49
  848.0 52.9 %copy-start.1 = (bf16[2048,512]{1,0:T(8,128)(2,1)S(1)}, bf16[2048,512]{1,0:T(8,128)(2,1)}, u32[]{:S(2)}) copy-start(bf16[2048,512]{1,0:T(8,128)(2,1)} %param.7) | copy-start | bytes 6291460
Sparse Core Ops, SparseCore 0:
  9.8 81.8 all-gather.6
  93.5 85.7 all-gather.4
  196.9 198.9 all-reduce.5
  406.2 101.8 reduce-scatter.3
  515.5 170.5 all-reduce.3
  687.8 70.8 all-gather.10
  761.0 86.9 all-gather.8
  851.1 25.6 reduce-scatter.5
  879.9 18.7 reduce-scatter.7
where the time goes:
time: 908 us; the launch traced here: 907 us
  waiting for transfers between devices  810 us (89%)
  matrix products  51.1 us (6%)
  local copies, waits for them, and re-layouts  25.7 us (3%)
  between operations  13.9 us (2%)
    psum x1, waiting for transfers between devices, on_device(): hidden_pre, hidden_grad = lax.psum((hidden_part, hgrad_part), 'chan')  199 us
    psum x1, waiting for transfers between devices, on_device(): time_rows = lax.psum(time_part, ('chan', 'dp'))  171 us
    reduce_scatter x1, waiting for transfers between devices, on_device(): lax.psum_scatter(jnp.einsum('rh,ch->rc', pre_grad, w_in, preferred_elemen...  101 us
    all_gather x1, waiting for transfers between devices, on_device(): all_gate = lax.all_gather(own_gate, 'tm', axis=0, tiled=True)  89.3 us
    all_gather x1, waiting for transfers between devices, on_device(): lax.all_gather(contexts, 'tm', axis=0, tiled=True)  83 us
    all_gather x1, waiting for transfers between devices, on_device(): lax.all_gather(cotangent, 'tm', axis=0, tiled=True)  61.4 us
    all_gather x1, waiting for transfers between devices, on_device(): grad_time = lax.all_gather(time_rows, 'tm', axis=0, tiled=True)  56.8 us
    reduce_scatter x1, waiting for transfers between devices, on_device(): lax.psum_scatter(win_part, 'dp', scatter_dimension=1, tiled=True)  24.6 us
  transfers between devices with their start and end apart: 9, of which 9 were waited for; matrix products, arithmetic and copies ran while one was open for 5% of the time, Pallas kernels for 0%

commit v1 on v0

--- a/solution.py
+++ b/solution.py
@@ -1,3 +1,4 @@
+import functools
 import math
 import jax
 import jax.numpy as jnp
@@ -6,6 +7,13 @@
 
 tanh_scale = math.sqrt(2.0 / math.pi)
 cubic_term = 0.044715
+
+
+def refer_frame(array_here, comm_axis):
+    return lax.all_gather(array_here, axis_name=comm_axis).sum(axis=0)
+
+
+apply_the_patch = functools.partial(refer_frame, comm_axis=("chan", "dp"))
 
 
 def gelu_pair(value):
@@ -69,7 +77,7 @@
         (mixed_grad + back).reshape(local_len, batch_dev, width_dev).astype(jnp.bfloat16)
     )
     time_part = jnp.einsum("tk,lk->tl", own_gate, flat_x, preferred_element_type=jnp.float32)
-    time_rows = lax.psum(time_part, ("chan", "dp"))
+    time_rows = apply_the_patch(time_part)
     grad_time = lax.all_gather(time_rows, "tm", axis=0, tiled=True)
     return (grad_contexts, grad_w_in, grad_w_out, grad_time)
 

time: 908 us -> 793 us (0.87)
  waiting for transfers between devices: 810 us -> 693 us
    psum x1 -> x0, waiting for transfers between devices: 171 us -> none  [on_device(): time_rows = lax.psum(time_part, ('chan', 'dp'))]
    all_gather x0 -> x1, waiting for transfers between devices: none -> 60.7 us  [refer_frame(): return lax.all_gather(array_here, axis_name=comm_axis).sum(axis=0)]
  transfers between devices with their start and end apart: 9 -> 9, of which waited for: 9 -> 9; matrix products, arithmetic and copies ran while one was open for 5% -> 6% of each run, Pallas kernels for 0% -> 0%
where the time goes in v1:
time: 793 us
  waiting for transfers between devices  693 us (87%)
  matrix products  51.1 us (6%)
  local copies, waits for them, and re-layouts  25.7 us (3%)
  between operations  13.9 us (2%)
  other arithmetic  8.28 us (1%)
    psum x1, waiting for transfers between devices, on_device(): hidden_pre, hidden_grad = lax.psum((hidden_part, hgrad_part), 'chan')  199 us
    reduce_scatter x1, waiting for transfers between devices, on_device(): lax.psum_scatter(jnp.einsum('rh,ch->rc', pre_grad, w_in, preferred_elemen...  101 us
    all_gather x1, waiting for transfers between devices, on_device(): all_gate = lax.all_gather(own_gate, 'tm', axis=0, tiled=True)  89.3 us
    all_gather x1, waiting for transfers between devices, on_device(): lax.all_gather(contexts, 'tm', axis=0, tiled=True)  83 us
    all_gather x1, waiting for transfers between devices, on_device(): lax.all_gather(cotangent, 'tm', axis=0, tiled=True)  61.4 us
    all_gather x1, waiting for transfers between devices, refer_frame(): return lax.all_gather(array_here, axis_name=comm_axis).sum(axis=0)  60.7 us
    all_gather x1, waiting for transfers between devices, on_device(): grad_time = lax.all_gather(time_rows, 'tm', axis=0, tiled=True)  50 us
    reduce_scatter x1, waiting for transfers between devices, on_device(): lax.psum_scatter(win_part, 'dp', scatter_dimension=1, tiled=True)  24.6 us
  transfers between devices with their start and end apart: 9, of which 9 were waited for; matrix products, arithmetic and copies ran while one was open for 6% of the time, Pallas kernels for 0%

profile of v1, /device:TPU:1, one launch (start us, length us, event | category | flops | bytes accessed | tf_op | source)
XLA Modules:
  0.0 792.6 jit_solution(6420958457680240411)
XLA Ops:
  7.2 0.0 copy-start
  7.2 0.0 all-gather.9.cloned.1.call-start
  7.2 0.7 all-gather.9.cloned.1.call-update
  7.9 0.0 all-gather.7.cloned.1.call-start
  8.0 0.7 all-gather.7.cloned.1.call-update
  8.7 0.0 all-reduce.3.cloned.1.call-start
  8.7 83.0 %all-gather.9.cloned.1.call-done = bf16[512,2,2048]{2,1,0:T(2,128)(2,1)} async-done(((bf16[32,2,2048]{2,1,0:T(2,128)(2,1)}), bf16[512,2,2048]{2,1,0:T(2,128)(2,1)}) %all-gather.9.cloned.1.call-update) | async-done | bytes 4194320 | tf_op jit(solution)/shard_map/all_gather | solution.py:36
  91.7 0.0 copy-start.9
  91.7 4.6 copy.9
  96.4 0.0 copy-start.2
  96.4 0.0 copy-done.9
  96.4 14.4 %fusion.1 = (f32[512,4096]{1,0:T(8,128)}, f32[512,4096]{1,0:T(8,128)}, bf16[512,4096]{1,0:T(8,128)(2,1)}, f32[512,4096]{1,0:T(8,128)}, f32[512,4096]{1,0:T(8,128)}) fusion(bf16[512,4096]{1,0:T(8,128)(2,1)S(1)} %bitcast.17, bf16[512,512]{1,0:T(8,128)(2,1)S(1)} %copy-done.9), kind=kOutput, calls=%fused_computation.2 | convolution fusion | flops 2170552320 | bytes 42467328 | tf_op jit(solution)/shard_map/dot_general | solution.py:41
  110.7 0.0 copy-done.2
  110.7 7.1 reshape.27
  117.9 61.4 %all-gather.7.cloned.1.call-done = bf16[512,2,2048]{2,1,0:T(2,128)(2,1)} async-done(((bf16[32,2,2048]{2,1,0:T(2,128)(2,1)}), bf16[512,2,2048]{2,1,0:T(2,128)(2,1)}) %all-gather.7.cloned.1.call-update) | async-done | bytes 4194320 | tf_op jit(solution)/shard_map/all_gather | solution.py:37
  179.3 7.2 reshape.25
  186.4 0.0 copy-start.3
  186.4 6.7 fusion.28
  193.1 0.0 copy-done
  193.1 0.0 copy-done.3
  193.1 3.7 fusion.29
  196.8 0.0 all-reduce.3.cloned.1.call-update
  196.8 0.2 reduce-scatter.4.cloned.1.call-start
  197.0 198.9 %all-reduce.3.cloned.1.call-done = (f32[1024,512]{1,0:T(8,128)}, f32[1024,512]{1,0:T(8,128)}) async-done(((f32[1024,512]{1,0:T(8,128)}, f32[1024,512]{1,0:T(8,128)}), (f32[1024,512]{1,0:T(8,128)}, f32[1024,512]{1,0:T(8,128)})) %all-reduce.3.cloned.1.call-update) | async-done | bytes 4194320 | tf_op jit(solution)/shard_map/psum | solution.py:51
  395.9 3.5 fusion.9
  399.5 0.0 copy-start.6
  399.5 1.0 copy-done.6
  400.4 5.6 fusion.30
  406.0 0.0 copy-start.8
  406.0 0.0 reduce-scatter.4.cloned.1.call-update
  406.1 0.0 all-gather.15.cloned.1.call-start
  406.1 0.9 copy-done.8
  407.0 0.1 reshape.29
  407.1 101.0 %reduce-scatter.4.cloned.1.call-done = f32[64,2048]{1,0:T(8,128)} async-done(((f32[1024,2048]{1,0:T(8,128)}), f32[64,2048]{1,0:T(8,128)}) %reduce-scatter.4.cloned.1.call-update) | async-done | bytes 524304 | tf_op jit(solution)/shard_map/reduce_scatter | solution.py:61
  508.0 1.1 add.56
  509.1 0.2 reshape.28
  509.3 1.7 fusion.19
  511.0 0.0 copy-start.4
  511.1 0.0 copy-start.7
  511.1 4.3 fusion.32
  515.4 0.0 copy-done.4
  515.4 0.0 all-gather.15.cloned.1.call-update
  515.4 0.0 all-gather.13.cloned.1.call-start
  515.4 60.7 %all-gather.15.cloned.1.call-done = f32[512,512]{1,0:T(8,128)} async-done(((f32[32,512]{1,0:T(8,128)}), f32[512,512]{1,0:T(8,128)}) %all-gather.15.cloned.1.call-update) | async-done | bytes 1048592 | tf_op jit(solution)/shard_map/all_gather | solution.py:13
  576.1 1.9 reduce_sum.9
  578.1 0.0 all-gather.13.cloned.1.call-update
  578.1 0.0 all-gather.11.cloned.1.call-start
  578.1 0.7 all-gather.11.cloned.1.call-update
  578.8 0.0 reduce-scatter.6.cloned.1.call-start
  578.9 0.0 copy-done.7
  578.9 6.6 fusion.31
  585.5 0.0 reduce-scatter.6.cloned.1.call-update
  585.5 0.0 reduce-scatter.8.cloned.1.call-start
  585.5 1.5 copy-done.5
  587.1 6.7 fusion.10
  593.8 0.0 reduce-scatter.8.cloned.1.call-update
  593.8 50.0 %all-gather.13.cloned.1.call-done = f32[512,512]{1,0:T(8,128)} async-done(((f32[32,512]{1,0:T(8,128)}), f32[512,512]{1,0:T(8,128)}) %all-gather.13.cloned.1.call-update) | async-done | bytes 1048592 | tf_op jit(solution)/shard_map/all_gather | solution.py:81
  643.8 89.3 %all-gather.11.cloned.1.call-done = bf16[512,4096]{1,0:T(8,128)(2,1)} async-done(((bf16[32,4096]{1,0:T(8,128)(2,1)}), bf16[512,4096]{1,0:T(8,128)(2,1)}) %all-gather.11.cloned.1.call-update) | async-done | bytes 4194320 | tf_op jit(solution)/shard_map/all_gather | solution.py:73
  733.1 3.3 fusion.2
  736.4 0.9 convert_element_type.34
  737.3 24.6 %reduce-scatter.6.cloned.1.call-done = f32[2048,256]{1,0:T(8,128)} async-done(((f32[2048,512]{1,0:T(8,128)}), f32[2048,256]{1,0:T(8,128)}) %reduce-scatter.6.cloned.1.call-update) | async-done | bytes 2097168 | tf_op jit(solution)/shard_map/reduce_scatter | solution.py:56
  761.9 21.9 %reduce-scatter.8.cloned.1.call-done = f32[256,2048]{1,0:T(8,128)} async-done(((f32[512,2048]{1,0:T(8,128)}), f32[256,2048]{1,0:T(8,128)}) %reduce-scatter.8.cloned.1.call-update) | async-done | bytes 2097168 | tf_op jit(solution)/shard_map/reduce_scatter | solution.py:57
  783.8 2.3 copy.13
  786.1 0.0 copy-done.1
  (2 shorter events, 0.0 us)
Async XLA Ops:
  7.2 186.0 %copy-start = (bf16[2048,512]{1,0:T(8,128)(2,1)S(1)}, bf16[2048,512]{1,0:T(8,128)(2,1)}, u32[]{:S(2)}) copy-start(bf16[2048,512]{1,0:T(8,128)(2,1)} %param.7) | copy-start | bytes 6291460
  7.2 84.5 %all-gather.9.cloned.1.call-start = ((), (), s32[]{:S(2)}) async-start(), calls=%async_computation.4 | async-start | bytes 4456448 | tf_op jit(solution)/shard_map/all_gather | solution.py:36
  7.9 171.3 %all-gather.7.cloned.1.call-start = ((), (), s32[]{:S(2)}) async-start(), calls=%async_computation.3 | async-start | bytes 4456448 | tf_op jit(solution)/shard_map/all_gather | solution.py:37
  8.7 387.2 %all-reduce.3.cloned.1.call-start = ((), (), s32[]{:S(2)}) async-start(), calls=%async_computation.11 | async-start | bytes 8388608 | tf_op jit(solution)/shard_map/psum | solution.py:51
  91.7 4.7 copy-start.9
  96.4 14.4 %copy-start.2 = (bf16[64,8,2,2048]{3,1,2,0:T(8,128)(2,1)}, bf16[64,8,2,2048]{3,1,2,0:T(8,128)(2,1)S(1)}, u32[]{:S(2)}) copy-start(bf16[64,8,2,2048]{3,1,2,0:T(8,128)(2,1)S(1)} %copy.9) | copy-start | bytes 12582916
  186.4 6.7 copy-start.3
  196.8 311.2 %reduce-scatter.4.cloned.1.call-start = ((), (), s32[]{:S(2)}) async-start(), calls=%async_computation.5 | async-start | bytes 8912896 | tf_op jit(solution)/shard_map/reduce_scatter | solution.py:61
  399.5 1.0 copy-start.6
  406.0 0.9 copy-start.8
  406.1 170.1 %all-gather.15.cloned.1.call-start = ((), (), s32[]{:S(2)}) async-start(), calls=%async_computation.10 | async-start | bytes 1114112 | tf_op jit(solution)/shard_map/all_gather | solution.py:13
  511.0 4.3 copy-start.4
  511.1 67.8 %copy-start.7 = (bf16[1024,512]{1,0:T(8,128)(2,1)S(1)}, bf16[1024,512]{1,0:T(8,128)(2,1)}, u32[]{:S(2)}) copy-start(bf16[1024,512]{1,0:T(8,128)(2,1)} %copy-done.6) | copy-start | bytes 3145732
  515.4 128.4 %all-gather.13.cloned.1.call-start = ((), (), s32[]{:S(2)}) async-start(), calls=%async_computation.9 | async-start | bytes 1114112 | tf_op jit(solution)/shard_map/all_gather | solution.py:81
  578.1 155.1 %all-gather.11.cloned.1.call-start = ((), (), s32[]{:S(2)}) async-start(), calls=%async_computation.6 | async-start | bytes 4456448 | tf_op jit(solution)/shard_map/all_gather | solution.py:73
  578.8 183.1 %reduce-scatter.6.cloned.1.call-start = ((), (), s32[]{:S(2)}) async-start(), calls=%async_computation.7 | async-start | bytes 6291456 | tf_op jit(solution)/shard_map/reduce_scatter | solution.py:56
  585.5 1.6 copy-start.5
  585.5 198.3 %reduce-scatter.8.cloned.1.call-start = ((), (), s32[]{:S(2)}) async-start(), calls=%async_computation.8 | async-start | bytes 6291456 | tf_op jit(solution)/shard_map/reduce_scatter | solution.py:57
  733.1 52.9 %copy-start.1 = (bf16[2048,512]{1,0:T(8,128)(2,1)S(1)}, bf16[2048,512]{1,0:T(8,128)(2,1)}, u32[]{:S(2)}) copy-start(bf16[2048,512]{1,0:T(8,128)(2,1)} %param.7) | copy-start | bytes 6291460
Sparse Core Ops, SparseCore 0:
  9.8 81.8 all-gather.8
  93.5 85.7 all-gather.6
  196.9 198.9 all-reduce.2
  406.2 101.8 reduce-scatter.3
  515.5 60.5 all-gather.14
  578.2 65.5 all-gather.12
  646.2 86.9 all-gather.10
  736.3 25.6 reduce-scatter.5
  765.0 18.7 reduce-scatter.7
